TPU v7x, 32 devices: a whole 2x2x4 slice. The times are simulated.
32 devices in a mesh: pw: 8 (over z, y), band: 4 (over x, core).
Axes of the slice: x: 2, y: 2, z: 4, core: 2. Of those that a mesh axis runs over, the one named last changes fastest.
Arguments:
- psi_block: float32 [2, 8, 256, 128], P(None, 'band', 'pw'), may hold values from -6 to 6
- psi_all: bfloat16 [2, 1024, 256, 128], P(None, 'band', 'pw'), may hold values from -0.0234375 to 0.0234375
- potential: float32 [128, 128, 128], P('pw'), may hold values from -8 to 8
- stick_col: int32 [256], replicated, may hold values from 0 to 16383, as said below
Outputs:
- intersection: float32 [2, 8, 1024], P(None, 'pw', 'band')
- hpsi: float32 [2, 8, 256, 128], P(None, 'band', 'pw')
Inputs may be any that keep to these rules, and one draw needn't show every extreme that they name: `stick_col`: distinct columns of the 128 x 128 plane; column 0 and column 16383 are always among them.
All inputs are finite; a program needn't handle non-finite values.
Results may differ from a plain program's by a relative error of at most 0.0029.
Values may be sent and summed in bfloat16 or wider, within the bound.
No kernel may reach another device: no remote copies, remote signals or barrier semaphores. Data moves between devices by JAX's collectives and lax.ppermute only.
A program may use at most 64 MiB of HBM per device.

v0:
```python
import math
import jax
import jax.numpy as jnp
from jax import lax
from jax.sharding import PartitionSpec as P


def frequency(index, size):
    return jnp.where(index < size // 2, index, index - size)


def kinetic_table(columns, grid_size):
    col_x = frequency(columns // grid_size, grid_size).astype(jnp.float32)
    col_y = frequency(columns % grid_size, grid_size).astype(jnp.float32)
    along = frequency(jnp.arange(grid_size, dtype=jnp.int32), grid_size).astype(jnp.float32)
    plane = col_x * col_x + col_y * col_y
    return 4.0 * (plane[:, None] + along[None, :] * along[None, :]) / float(grid_size * grid_size)


def dft_table(grid_size, sign):
    indices = jnp.arange(grid_size, dtype=jnp.int32)
    products = indices[:, None] * indices[None, :] % grid_size
    angles = 2.0 * math.pi / grid_size * products.astype(jnp.float32)
    cosine = jnp.cos(angles)
    sine = sign * jnp.sin(angles)
    return jnp.stack([jnp.stack([cosine, -sine]), jnp.stack([sine, cosine])])


def per_device(psi_block, psi_all, potential, stick_col):
    local_bands = psi_block.shape[1]
    sticks_dev = psi_block.shape[2]
    grid_size = psi_block.shape[3]
    highest = lax.Precision.HIGHEST
    rank = lax.axis_index("pw")
    pw_count = lax.axis_size("pw")
    band_count = lax.axis_size("band")
    my_columns = lax.dynamic_slice_in_dim(stick_col, rank * sticks_dev, sticks_dev)
    kinetic = kinetic_table(my_columns, grid_size)
    inverse = dft_table(grid_size, 1.0)
    forward = dft_table(grid_size, -1.0)
    cosine = inverse[0, 0]
    sine = inverse[1, 0]
    grid_iota = jnp.arange(grid_size, dtype=jnp.int32)
    col_x = stick_col // grid_size
    col_y = stick_col % grid_size
    phase_angles = (
        2.0
        * math.pi
        / grid_size
        * (grid_iota[:, None] * col_y[None, :] % grid_size).astype(jnp.float32)
    )
    phase_cos = jnp.cos(phase_angles)
    phase_sin = jnp.sin(phase_angles)
    place_rows = (col_x[:, None] == grid_iota[None, :]).astype(jnp.float32)
    pick_rows = (grid_iota[:, None] == col_x[None, :]).astype(jnp.float32)
    turned_pot = (jnp.transpose(potential, (0, 2, 1)) / float(grid_size**3))[None]

    def mult(left, right):
        return jnp.dot(left, right, precision=highest, preferred_element_type=jnp.float32)

    all_re = psi_all[0].reshape(psi_all.shape[1], -1)
    all_im = psi_all[1].reshape(psi_all.shape[1], -1)
    dims = (((1,), (1,)), ((), ()))
    group_count = local_bands // 2
    z_lines = jnp.einsum("dcvu,cbsu->bvds", inverse, psi_block, precision=highest)
    planes_in = lax.all_to_all(z_lines, "pw", split_axis=1, concat_axis=3, tiled=True)
    val_re = planes_in[:, :, 0, None, :]
    val_im = planes_in[:, :, 1, None, :]
    spread_re = val_re * phase_cos - val_im * phase_sin
    spread_im = val_re * phase_sin + val_im * phase_cos
    rows_re = mult(spread_re, place_rows)
    rows_im = mult(spread_im, place_rows)
    wave_re = (mult(rows_re, cosine) - mult(rows_im, sine)) * turned_pot
    wave_im = (mult(rows_re, sine) + mult(rows_im, cosine)) * turned_pot
    back_re = mult(wave_re, cosine) + mult(wave_im, sine)
    back_im = mult(wave_im, cosine) - mult(wave_re, sine)
    sel_re = mult(back_re, pick_rows)
    sel_im = mult(back_im, pick_rows)
    picked_re = jnp.sum(sel_re * phase_cos + sel_im * phase_sin, axis=2)
    picked_im = jnp.sum(sel_im * phase_cos - sel_re * phase_sin, axis=2)
    picked = jnp.stack([picked_re, picked_im], axis=2)
    sticks_back = lax.all_to_all(picked, "pw", split_axis=3, concat_axis=1, tiled=True)
    vpsi = jnp.einsum("dcvu,bucs->dbsv", forward, sticks_back, precision=highest)
    applied = kinetic[None, None] * psi_block + vpsi
    lowered = applied.astype(jnp.bfloat16)
    gathered = lax.all_gather(lowered, "band", axis=1, tiled=True)
    h_re = gathered[0].reshape(gathered.shape[1], -1)
    h_im = gathered[1].reshape(gathered.shape[1], -1)
    real_part = lax.dot_general(
        h_re, all_re, dims, preferred_element_type=jnp.float32
    ) + lax.dot_general(h_im, all_im, dims, preferred_element_type=jnp.float32)
    imag_part = lax.dot_general(
        h_re, all_im, dims, preferred_element_type=jnp.float32
    ) - lax.dot_general(h_im, all_re, dims, preferred_element_type=jnp.float32)
    partials = [jnp.stack([real_part, imag_part])]
    stacked = jnp.stack(partials, axis=1)
    stacked = stacked.reshape(2, group_count, band_count, 2, stacked.shape[-1])
    partial_value = jnp.transpose(stacked, (0, 2, 1, 3, 4)).reshape(
        2, band_count * local_bands, stacked.shape[-1]
    )
    summed = lax.psum(partial_value, "pw")
    cols_dev = partial_value.shape[1] // pw_count
    intersection = lax.dynamic_slice_in_dim(summed, rank * cols_dev, cols_dev, 1)
    return (intersection, applied)


def solution(mesh):
    return jax.shard_map(
        per_device,
        mesh=mesh,
        in_specs=(
            P(None, "band", "pw", None),
            P(None, "band", "pw", None),
            P("pw", None, None),
            P(),
        ),
        out_specs=(P(None, "pw", "band"), P(None, "band", "pw", None)),
        check_vma=False,
    )
```

profile of v0, /device:TPU:0, one launch (start us, length us, event | category | flops | bytes accessed | tf_op | source)
XLA Modules:
  0.0 115.9 jit_solution(15763958665738720233)
XLA Ops:
  2.2 1.2 %convolution_bitcast_fusion = f32[2,128,2,32]{1,3,0,2:T(8,128)S(1)} fusion(f32[1,2,128,128]{3,2,1,0:T(8,128)S(1)} %get-tuple-element.20, f32[1,2,128,128]{3,2,1,0:T(8,128)S(1)} %get-tuple-element.21, f32[2,2,32,128]{3,2,1,0:T(8,128)} %param.4), kind=kOutput, calls=%fused_computation.30 | convolution fusion | flops 50397184 | bytes 393216 | tf_op jit(solution)/shard_map/dcvu,cbsu->bvds/dot_general | solution.py:65
  3.6 0.9 reshape.230
  4.5 7.3 %all-to-all-start = ((f32[8,1,2048]{2,1,0:T(1,128)}), f32[8,1,2048]{2,1,0:T(1,128)}, u32[]{:S(2)}, u32[]{:S(2)}) async-start(f32[8,1,2048]{2,1,0:T(1,128)} %reshape.230), calls=%async_computation | async-start | bytes 131072 | tf_op jit(solution)/shard_map/all_to_all | solution.py:66
  11.8 1.2 %fusion.62 = (f32[128,256]{1,0:T(8,128)S(1)}, f32[128,256]{1,0:T(8,128)}) fusion(s32[256]{0:T(256)S(1)} %get-tuple-element.25), kind=kLoop, calls=%fused_computation.86 | loop fusion | flops 458752 | bytes 263168 | tf_op jit(solution)/shard_map/cos | solution.py:52
  13.0 1.1 multiply_bitcast_fusion
  14.1 4.3 %fusion.86 = (bf16[1,256,32,128]{3,2,1,0:T(8,128)(2,1)S(1)}, bf16[1,256,32,128]{3,2,1,0:T(8,128)(2,1)}) fusion(bf16[2,256,32,128]{3,2,1,0:T(8,128)(2,1)} %param.5), kind=kLoop, calls=%fused_computation.131 | loop fusion | bytes 8388608 | tf_op jit(solution)/shard_map/slice | solution.py:61
  18.4 1.6 %copy.66 = f32[16,128,128]{2,1,0:T(8,128)S(1)} copy(f32[16,128,128]{1,2,0:T(8,128)} %multiply_bitcast_fusion) | data formatting | bytes 2097152 | tf_op jit(solution)/shard_map/div | solution.py:56
  20.6 2.3 %reduce = f32[8,2048]{1,0:T(8,128)} reduce(f32[8,1,2048]{2,1,0:T(1,128)} %all-to-all-done, f32[]{:T(128)} %broadcast.384), dimensions={1}, to_apply=%all_to_all.26.reduce_sub_computation | reduce | bytes 131076 | tf_op jit(solution)/shard_map/all_to_all | solution.py:66
  22.8 1.8 %reshape.231 = f32[128,2,2,32]{3,2,1,0:T(2,128)} reshape(f32[8,2048]{1,0:T(8,128)} %reduce) | data formatting | bytes 131072
  24.6 1.0 copy.64
  25.6 0.8 copy.65
  26.4 1.7 %all_to_all.29 = f32[2,16,2,256]{3,1,2,0:T(8,128)} reshape(f32[2,16,2,8,32]{4,3,1,2,0:T(8,128)} %copy.65) | data formatting | bytes 131072 | tf_op jit(solution)/shard_map/all_to_all | solution.py:66
  28.1 0.8 slice_bitcast_fusion.11
  28.9 3.3 %fusion = f32[2,16,128,128]{3,2,1,0:T(8,128)S(1)} fusion(f32[128,256]{1,0:T(8,128)} %get-tuple-element.27, f32[2,16,256]{2,1,0:T(8,128)S(1)} %get-tuple-element.23, f32[128,256]{1,0:T(8,128)S(1)} %get-tuple-element.26, f32[2,16,256]{2,1,0:T(8,128)S(1)} %get-tuple-element.22, s32[256]{0:T(256)S(1)} %get-tuple-element.24), kind=kOutput, calls=%fused_computation.2 | convolution fusion | flops 1613791232 | bytes 2425856 | tf_op jit(solution)/shard_map/dot_general | solution.py:59
  32.3 2.5 %fusion.4 = f32[2,16,128,128]{3,2,1,0:T(8,128)S(1)} fusion(f32[128,256]{1,0:T(8,128)S(1)} %copy-done.1, f32[2,16,256]{2,1,0:T(8,128)S(1)} %get-tuple-element.23, f32[128,256]{1,0:T(8,128)S(1)} %get-tuple-element.26, f32[2,16,256]{2,1,0:T(8,128)S(1)} %get-tuple-element.22, s32[256]{0:T(256)S(1)} %get-tuple-element.24), kind=kOutput, calls=%fused_computation.6 | convolution fusion | flops 1613791232 | bytes 2425856 | tf_op jit(solution)/shard_map/dot_general | solution.py:59
  34.7 1.9 %fusion.72 = f32[2,16,128,128]{3,2,1,0:T(8,128)S(1)} fusion(f32[2,16,128,128]{3,2,1,0:T(8,128)S(1)} %fusion.4, f32[1,2,128,128]{3,2,1,0:T(8,128)S(1)} %get-tuple-element.20), kind=kOutput, calls=%fused_computation.96 | convolution fusion | flops 805306368 | bytes 4259840 | tf_op jit(solution)/shard_map/dot_general | solution.py:59
  36.6 1.8 %fusion.69 = f32[2,16,128,128]{3,2,1,0:T(8,128)S(1)} fusion(f32[2,16,128,128]{3,2,1,0:T(8,128)S(1)} %fusion.4, f32[1,2,128,128]{3,2,1,0:T(8,128)S(1)} %get-tuple-element.21), kind=kOutput, calls=%fused_computation.93 | convolution fusion | flops 805306368 | bytes 4259840 | tf_op jit(solution)/shard_map/dot_general | solution.py:59
  38.4 2.0 %subtract_multiply_fusion = f32[2,16,128,128]{3,2,1,0:T(8,128)S(1)} fusion(f32[2,16,128,128]{3,2,1,0:T(8,128)S(1)} %fusion.69, f32[2,16,128,128]{3,2,1,0:T(8,128)S(1)} %fusion, f32[16,128,128]{2,1,0:T(8,128)S(1)} %copy.66, f32[1,2,128,128]{3,2,1,0:T(8,128)S(1)} %get-tuple-element.20), kind=kOutput, calls=%fused_computation.17 | convolution fusion | flops 806354944 | bytes 7405568 | tf_op jit(solution)/shard_map/dot_general | solution.py:59
  40.4 1.8 %fusion.70 = f32[2,16,128,128]{3,2,1,0:T(8,128)S(1)} fusion(f32[2,16,128,128]{3,2,1,0:T(8,128)S(1)} %subtract_multiply_fusion, f32[1,2,128,128]{3,2,1,0:T(8,128)S(1)} %get-tuple-element.20), kind=kOutput, calls=%fused_computation.94 | convolution fusion | flops 805306368 | bytes 4259840 | tf_op jit(solution)/shard_map/dot_general | solution.py:59
  42.2 1.8 %fusion.68 = f32[2,16,128,128]{3,2,1,0:T(8,128)S(1)} fusion(f32[2,16,128,128]{3,2,1,0:T(8,128)S(1)} %subtract_multiply_fusion, f32[1,2,128,128]{3,2,1,0:T(8,128)S(1)} %get-tuple-element.21), kind=kOutput, calls=%fused_computation.92 | convolution fusion | flops 805306368 | bytes 4259840 | tf_op jit(solution)/shard_map/dot_general | solution.py:59
  44.0 1.9 %add_multiply_fusion = f32[2,16,128,128]{3,2,1,0:T(8,128)S(1)} fusion(f32[2,16,128,128]{3,2,1,0:T(8,128)S(1)} %fusion.72, f32[2,16,128,128]{3,2,1,0:T(8,128)S(1)} %fusion, f32[16,128,128]{2,1,0:T(8,128)S(1)} %copy.66, f32[1,2,128,128]{3,2,1,0:T(8,128)S(1)} %get-tuple-element.21), kind=kOutput, calls=%fused_computation.16 | convolution fusion | flops 806354944 | bytes 7405568 | tf_op jit(solution)/shard_map/dot_general | solution.py:59
  46.0 1.8 %fusion.67 = f32[2,16,128,128]{3,2,1,0:T(8,128)S(1)} fusion(f32[2,16,128,128]{3,2,1,0:T(8,128)S(1)} %add_multiply_fusion, f32[1,2,128,128]{3,2,1,0:T(8,128)S(1)} %get-tuple-element.21), kind=kOutput, calls=%fused_computation.91 | convolution fusion | flops 805306368 | bytes 4259840 | tf_op jit(solution)/shard_map/dot_general | solution.py:59
  47.7 1.8 %fusion.71 = f32[2,16,128,128]{3,2,1,0:T(8,128)S(1)} fusion(f32[2,16,128,128]{3,2,1,0:T(8,128)S(1)} %add_multiply_fusion, f32[1,2,128,128]{3,2,1,0:T(8,128)S(1)} %get-tuple-element.20), kind=kOutput, calls=%fused_computation.95 | convolution fusion | flops 805306368 | bytes 4259840 | tf_op jit(solution)/shard_map/dot_general | solution.py:59
  49.6 1.8 %fusion.10 = f32[2,16,128,256]{3,2,1,0:T(8,128)S(1)} fusion(f32[2,16,128,128]{3,2,1,0:T(8,128)S(1)} %fusion.68, f32[2,16,128,128]{3,2,1,0:T(8,128)S(1)} %fusion.71, s32[256]{0:T(256)S(1)} %get-tuple-element.24), kind=kOutput, calls=%fused_computation.14 | convolution fusion | flops 1611169792 | bytes 8389632 | tf_op jit(solution)/shard_map/dot_general | solution.py:59
  51.4 2.8 %add_reduce_fusion = (f32[2,16,256]{2,1,0:T(8,128)S(1)}, f32[2,16,256]{2,1,0:T(8,128)S(1)}) fusion(f32[2,16,128,256]{3,2,1,0:T(8,128)S(1)} %fusion.10, f32[128,256]{1,0:T(8,128)S(1)} %copy-done.1, f32[128,256]{1,0:T(8,128)S(1)} %get-tuple-element.26, s32[256]{0:T(256)S(1)} %get-tuple-element.24, f32[2,16,128,128]{3,2,1,0:T(8,128)S(1)} %fusion.67, ...), kind=kOutput, calls=%fused_computation.1 | convolution fusion | flops 1619542016 | bytes 8717312 | tf_op jit(solution)/shard_map/dot_general | solution.py:59
  54.5 1.4 %reshape.232 = f32[8,1,2048]{2,1,0:T(1,128)} reshape(f32[256,2,2,16]{3,2,1,0:T(2,128)S(1)} %bitcast.156) | data formatting | bytes 131072
  55.9 6.0 %all-to-all-start.1 = ((f32[8,1,2048]{2,1,0:T(1,128)}), f32[8,1,2048]{2,1,0:T(1,128)S(1)}, u32[]{:S(2)}, u32[]{:S(2)}) async-start(f32[8,1,2048]{2,1,0:T(1,128)} %reshape.232), calls=%async_computation.1 | async-start | bytes 131072 | tf_op jit(solution)/shard_map/all_to_all | solution.py:82
  62.0 6.8 %all-to-all-done.1 = f32[8,1,2048]{2,1,0:T(1,128)S(1)} async-done(((f32[8,1,2048]{2,1,0:T(1,128)}), f32[8,1,2048]{2,1,0:T(1,128)S(1)}, u32[]{:S(2)}, u32[]{:S(2)}) %all-to-all-start.1) | async-done | bytes 65568 | tf_op jit(solution)/shard_map/all_to_all | solution.py:82
  68.8 0.8 reduce.1
  71.9 5.4 %all_gather.3 = bf16[2,8,32,128]{3,2,0,1:T(8,128)(2,1)S(1)} all-gather(bf16[2,2,32,128]{3,2,0,1:T(8,128)(2,1)S(1)} %get-tuple-element.28), channel_id=1, replica_groups=mesh['pw'=8,'band'=4] {'band'}, dimensions={1}, use_global_device_ids=true | all-gather | bytes 163840 | tf_op jit(solution)/shard_map/all_gather | solution.py:86
  77.3 2.3 %fusion.26 = f32[8,256]{1,0:T(8,128)S(1)} fusion(bf16[1,256,32,128]{3,2,1,0:T(8,128)(2,1)} %get-tuple-element.15, bf16[1,8,32,128]{3,2,0,1:T(8,128)(2,1)S(1)} %get-tuple-element.17), kind=kOutput, calls=%fused_computation.34 | convolution fusion | flops 16777216 | bytes 2170880 | tf_op jit(solution)/shard_map/dot_general | solution.py:92
  81.7 33.7 %psum.7 = f32[2,8,256]{2,1,0:T(8,128)S(1)} all-reduce(f32[2,8,256]{2,1,0:T(8,128)S(1)} %pad_maximum_fusion.5), channel_id=1, replica_groups=mesh['pw'=8,'band'=4] {'pw'}, use_global_device_ids=true, to_apply=%region_2.3 | all-reduce | flops 4096 | bytes 32768 | tf_op jit(solution)/shard_map/psum | solution.py:101
  (37 shorter events, 7.7 us)
Async XLA Ops:
  0.6 11.2 %copy-start.6 = (s32[256]{0:T(256)S(1)}, s32[256]{0:T(256)}, u32[]{:S(2)}) copy-start(s32[256]{0:T(256)} %param.7) | copy-start | bytes 3076
  0.6 12.4 %copy-start.2 = (f32[16,128,128]{2,1,0:T(8,128)S(1)}, f32[16,128,128]{2,1,0:T(8,128)}, u32[]{:S(2)}) copy-start(f32[16,128,128]{2,1,0:T(8,128)} %param.6) | copy-start | bytes 3145732
  4.5 15.5 %all-to-all-start = ((f32[8,1,2048]{2,1,0:T(1,128)}), f32[8,1,2048]{2,1,0:T(1,128)}, u32[]{:S(2)}, u32[]{:S(2)}) async-start(f32[8,1,2048]{2,1,0:T(1,128)} %reshape.230), calls=%async_computation | async-start | bytes 131072 | tf_op jit(solution)/shard_map/all_to_all | solution.py:66
  28.1 4.2 %copy-start.1 = (f32[128,256]{1,0:T(8,128)S(1)}, f32[128,256]{1,0:T(8,128)}, u32[]{:S(2)}) copy-start(f32[128,256]{1,0:T(8,128)} %get-tuple-element.27) | copy-start | bytes 393220
  54.2 16.5 %copy-start.3 = (f32[1,2,128,128]{3,2,1,0:T(8,128)S(1)}, f32[1,2,128,128]{3,2,1,0:T(8,128)}, u32[]{:S(2)}) copy-start(f32[1,2,128,128]{3,2,1,0:T(8,128)} %get-tuple-element.18) | copy-start | bytes 393220
  54.2 16.5 %copy-start.4 = (f32[1,2,128,128]{3,2,1,0:T(8,128)S(1)}, f32[1,2,128,128]{3,2,1,0:T(8,128)}, u32[]{:S(2)}) copy-start(f32[1,2,128,128]{3,2,1,0:T(8,128)} %get-tuple-element.19) | copy-start | bytes 393220
  54.2 16.5 %copy-start.5 = (f32[2,2,32,128]{3,2,1,0:T(8,128)S(1)}, f32[2,2,32,128]{3,2,1,0:T(8,128)}, u32[]{:S(2)}) copy-start(f32[2,2,32,128]{3,2,1,0:T(8,128)} %param.4) | copy-start | bytes 196612
  55.9 12.9 %all-to-all-start.1 = ((f32[8,1,2048]{2,1,0:T(1,128)}), f32[8,1,2048]{2,1,0:T(1,128)S(1)}, u32[]{:S(2)}, u32[]{:S(2)}) async-start(f32[8,1,2048]{2,1,0:T(1,128)} %reshape.232), calls=%async_computation.1 | async-start | bytes 131072 | tf_op jit(solution)/shard_map/all_to_all | solution.py:82
  70.6 9.0 %copy-start = (bf16[1,256,32,128]{3,2,1,0:T(8,128)(2,1)S(1)}, bf16[1,256,32,128]{3,2,1,0:T(8,128)(2,1)}, u32[]{:S(2)}) copy-start(bf16[1,256,32,128]{3,2,1,0:T(8,128)(2,1)} %get-tuple-element.15) | copy-start | bytes 6291460
where the time goes:
time: 117 us; the launch traced here: 116 us
  blocking collectives  39.1 us (33%)
  matrix products  31.3 us (27%)
  local copies, waits for them, and re-layouts  17.5 us (15%)
  starting transfers between devices  13.3 us (11%)
  other arithmetic  7.07 us (6%)
  waiting for transfers between devices  6.84 us (6%)
    psum x1, blocking collectives, per_device(): summed = lax.psum(partial_value, 'pw')  33.7 us
    dot_general x12, matrix products, mult(): jnp.dot(left, right, precision=highest, preferred_element_type=jnp.float32)  25.2 us
    all_to_all x1, starting transfers between devices, per_device(): lax.all_to_all(z_lines, 'pw', split_axis=1, concat_axis=3, tiled=True)  7.28 us
    all_to_all x1, waiting for transfers between devices, per_device(): lax.all_to_all(picked, 'pw', split_axis=3, concat_axis=1, tiled=True)  6.83 us
    all_to_all x1, starting transfers between devices, per_device(): lax.all_to_all(picked, 'pw', split_axis=3, concat_axis=1, tiled=True)  5.99 us
    unnamed x19, local copies, waits for them, and re-layouts  5.42 us
    all_gather x1, blocking collectives, per_device(): gathered = lax.all_gather(lowered, 'band', axis=1, tiled=True)  5.41 us
    slice x1, local copies, waits for them, and re-layouts, per_device(): all_re = psi_all[0].reshape(psi_all.shape[1], -1)  4.29 us
  transfers between devices with their start and end apart: 2, of which 1 were waited for; matrix products, arithmetic and copies ran while one was open for 7% of the time, Pallas kernels for 0%

commit v1 on v0

--- a/solution.py
+++ b/solution.py
@@ -3,6 +3,16 @@
 import jax.numpy as jnp
 from jax import lax
 from jax.sharding import PartitionSpec as P
+
+
+def pass_along(block, axis, d):
+    devices = lax.axis_size(axis)
+    moving, blocks = (block, [block])
+    for _ in range(devices - 1):
+        moving = lax.ppermute(moving, axis, [(i, (i + 1) % devices) for i in range(devices)])
+        blocks.insert(0, moving)
+    line = jnp.concatenate(blocks, axis=d)
+    return jnp.roll(line, (lax.axis_index(axis) + 1) * block.shape[d], axis=d)
 
 
 def frequency(index, size):
@@ -83,7 +93,7 @@
     vpsi = jnp.einsum("dcvu,bucs->dbsv", forward, sticks_back, precision=highest)
     applied = kinetic[None, None] * psi_block + vpsi
     lowered = applied.astype(jnp.bfloat16)
-    gathered = lax.all_gather(lowered, "band", axis=1, tiled=True)
+    gathered = pass_along(lowered, "band", 1)
     h_re = gathered[0].reshape(gathered.shape[1], -1)
     h_im = gathered[1].reshape(gathered.shape[1], -1)
     real_part = lax.dot_general(

time: 117 us -> 109 us (0.932); the launches traced: 116 us -> 109 us
  waiting for transfers between devices: 6.84 us -> 19.2 us
  local copies, waits for them, and re-layouts: 17.5 us -> 10.7 us
  blocking collectives: 39.1 us -> 33.7 us
  other arithmetic: 7.07 us -> 3.25 us
  starting transfers between devices: 13.3 us -> 10.7 us
    ppermute x0 -> x3, waiting for transfers between devices: none -> 6.67 us  [pass_along(): lax.ppermute(moving, axis, [(i, (i + 1) % devices) for i in range(devices)])]
    all_to_all x1, waiting for transfers between devices: 0.01 us -> 5.79 us  [per_device(): lax.all_to_all(z_lines, 'pw', split_axis=1, concat_axis=3, tiled=True)]
    all_gather x1 -> x0, blocking collectives: 5.41 us -> none  [per_device(): gathered = lax.all_gather(lowered, 'band', axis=1, tiled=True)]
    all_to_all x4, local copies, waits for them, and re-layouts: 3.97 us -> 0.74 us  [per_device(): lax.all_to_all(z_lines, 'pw', split_axis=1, concat_axis=3, tiled=True)]
    all_to_all x1, starting transfers between devices: 5.99 us -> 3.35 us  [per_device(): lax.all_to_all(picked, 'pw', split_axis=3, concat_axis=1, tiled=True)]
    unnamed x19 -> x20, local copies, waits for them, and re-layouts: 5.42 us -> 3.93 us
    all_to_all x1, other arithmetic: 2.27 us -> 0.8 us  [per_device(): lax.all_to_all(z_lines, 'pw', split_axis=1, concat_axis=3, tiled=True)]
    div x1, local copies, waits for them, and re-layouts: 1.55 us -> 0.33 us  [per_device(): jnp.transpose(potential, (0, 2, 1)) / float(grid_size ** 3)]
  transfers between devices with their start and end apart: 2 -> 5, of which waited for: 1 -> 4; matrix products, arithmetic and copies ran while one was open for 7% -> 6% of each run, Pallas kernels for 0% -> 0%
where the time goes in v1:
time: 109 us
  blocking collectives  33.7 us (31%)
  matrix products  30.6 us (28%)
  waiting for transfers between devices  19.2 us (18%)
  local copies, waits for them, and re-layouts  10.7 us (10%)
  starting transfers between devices  10.7 us (10%)
  other arithmetic  3.25 us (3%)
    psum x1, blocking collectives, per_device(): summed = lax.psum(partial_value, 'pw')  33.7 us
    dot_general x12, matrix products, mult(): jnp.dot(left, right, precision=highest, preferred_element_type=jnp.float32)  24.4 us
    all_to_all x1, starting transfers between devices, per_device(): lax.all_to_all(z_lines, 'pw', split_axis=1, concat_axis=3, tiled=True)  7.28 us
    all_to_all x1, waiting for transfers between devices, per_device(): lax.all_to_all(picked, 'pw', split_axis=3, concat_axis=1, tiled=True)  6.77 us
    ppermute x3, waiting for transfers between devices, pass_along(): lax.ppermute(moving, axis, [(i, (i + 1) % devices) for i in range(devices)])  6.67 us
    all_to_all x1, waiting for transfers between devices, per_device(): lax.all_to_all(z_lines, 'pw', split_axis=1, concat_axis=3, tiled=True)  5.79 us
    slice x1, local copies, waits for them, and re-layouts, per_device(): all_re = psi_all[0].reshape(psi_all.shape[1], -1)  4.3 us
    unnamed x20, local copies, waits for them, and re-layouts  3.93 us
  transfers between devices with their start and end apart: 5, of which 4 were waited for; matrix products, arithmetic and copies ran while one was open for 6% of the time, Pallas kernels for 0%

profile of v1, /device:TPU:0, one launch (start us, length us, event | category | flops | bytes accessed | tf_op | source)
XLA Modules:
  0.0 109.1 jit_solution(3867865892417051587)
XLA Ops:
  1.5 1.2 %convolution_bitcast_fusion = f32[2,128,2,32]{1,3,0,2:T(8,128)S(1)} fusion(f32[1,2,128,128]{3,2,1,0:T(8,128)S(1)} %get-tuple-element.20, f32[1,2,128,128]{3,2,1,0:T(8,128)S(1)} %get-tuple-element.21, f32[2,2,32,128]{3,2,1,0:T(8,128)} %param.4), kind=kOutput, calls=%fused_computation.30 | convolution fusion | flops 50397184 | bytes 393216 | tf_op jit(solution)/shard_map/dcvu,cbsu->bvds/dot_general | solution.py:75
  2.9 0.9 reshape.230
  3.8 7.3 %all-to-all-start = ((f32[8,1,2048]{2,1,0:T(1,128)}), f32[8,1,2048]{2,1,0:T(1,128)S(1)}, u32[]{:S(2)}, u32[]{:S(2)}) async-start(f32[8,1,2048]{2,1,0:T(1,128)} %reshape.230), calls=%async_computation | async-start | bytes 131072 | tf_op jit(solution)/shard_map/all_to_all | solution.py:76
  12.2 5.8 %all-to-all-done = f32[8,1,2048]{2,1,0:T(1,128)S(1)} async-done(((f32[8,1,2048]{2,1,0:T(1,128)}), f32[8,1,2048]{2,1,0:T(1,128)S(1)}, u32[]{:S(2)}, u32[]{:S(2)}) %all-to-all-start) | async-done | bytes 65568 | tf_op jit(solution)/shard_map/all_to_all | solution.py:76
  18.5 0.8 reduce
  19.8 2.4 %fusion = f32[2,16,128,128]{3,2,1,0:T(8,128)S(1)} fusion(f32[128,256]{1,0:T(8,128)S(1)} %get-tuple-element.27, f32[2,16,256]{2,1,0:T(8,128)S(1)} %get-tuple-element.23, f32[128,256]{1,0:T(8,128)S(1)} %get-tuple-element.26, f32[2,16,256]{2,1,0:T(8,128)S(1)} %get-tuple-element.22, s32[256]{0:T(256)S(1)} %get-tuple-element.24), kind=kOutput, calls=%fused_computation.2 | convolution fusion | flops 1613791232 | bytes 2425856 | tf_op jit(solution)/shard_map/dot_general | solution.py:69
  22.3 2.4 %fusion.4 = f32[2,16,128,128]{3,2,1,0:T(8,128)S(1)} fusion(f32[128,256]{1,0:T(8,128)S(1)} %get-tuple-element.27, f32[2,16,256]{2,1,0:T(8,128)S(1)} %get-tuple-element.23, f32[128,256]{1,0:T(8,128)S(1)} %get-tuple-element.26, f32[2,16,256]{2,1,0:T(8,128)S(1)} %get-tuple-element.22, s32[256]{0:T(256)S(1)} %get-tuple-element.24), kind=kOutput, calls=%fused_computation.6 | convolution fusion | flops 1613791232 | bytes 2425856 | tf_op jit(solution)/shard_map/dot_general | solution.py:69
  24.7 1.8 %fusion.76 = f32[2,16,128,128]{3,2,1,0:T(8,128)S(1)} fusion(f32[2,16,128,128]{3,2,1,0:T(8,128)S(1)} %fusion.4, f32[1,2,128,128]{3,2,1,0:T(8,128)S(1)} %get-tuple-element.20), kind=kOutput, calls=%fused_computation.100 | convolution fusion | flops 805306368 | bytes 4259840 | tf_op jit(solution)/shard_map/dot_general | solution.py:69
  26.6 1.8 %fusion.73 = f32[2,16,128,128]{3,2,1,0:T(8,128)S(1)} fusion(f32[2,16,128,128]{3,2,1,0:T(8,128)S(1)} %fusion.4, f32[1,2,128,128]{3,2,1,0:T(8,128)S(1)} %get-tuple-element.21), kind=kOutput, calls=%fused_computation.97 | convolution fusion | flops 805306368 | bytes 4259840 | tf_op jit(solution)/shard_map/dot_general | solution.py:69
  28.4 1.9 %subtract_multiply_fusion = f32[2,16,128,128]{3,2,1,0:T(8,128)S(1)} fusion(f32[2,16,128,128]{3,2,1,0:T(8,128)S(1)} %fusion.73, f32[2,16,128,128]{3,2,1,0:T(8,128)S(1)} %fusion, f32[16,128,128]{2,1,0:T(8,128)S(1)} %copy.70, f32[1,2,128,128]{3,2,1,0:T(8,128)S(1)} %get-tuple-element.20), kind=kOutput, calls=%fused_computation.17 | convolution fusion | flops 806354944 | bytes 7405568 | tf_op jit(solution)/shard_map/dot_general | solution.py:69
  30.4 2.0 %fusion.74 = f32[2,16,128,128]{3,2,1,0:T(8,128)S(1)} fusion(f32[2,16,128,128]{3,2,1,0:T(8,128)S(1)} %subtract_multiply_fusion, f32[1,2,128,128]{3,2,1,0:T(8,128)S(1)} %get-tuple-element.20), kind=kOutput, calls=%fused_computation.98 | convolution fusion | flops 805306368 | bytes 4259840 | tf_op jit(solution)/shard_map/dot_general | solution.py:69
  32.4 1.8 %fusion.72 = f32[2,16,128,128]{3,2,1,0:T(8,128)S(1)} fusion(f32[2,16,128,128]{3,2,1,0:T(8,128)S(1)} %subtract_multiply_fusion, f32[1,2,128,128]{3,2,1,0:T(8,128)S(1)} %get-tuple-element.21), kind=kOutput, calls=%fused_computation.96 | convolution fusion | flops 805306368 | bytes 4259840 | tf_op jit(solution)/shard_map/dot_general | solution.py:69
  34.2 1.9 %add_multiply_fusion = f32[2,16,128,128]{3,2,1,0:T(8,128)S(1)} fusion(f32[2,16,128,128]{3,2,1,0:T(8,128)S(1)} %fusion.76, f32[2,16,128,128]{3,2,1,0:T(8,128)S(1)} %fusion, f32[16,128,128]{2,1,0:T(8,128)S(1)} %copy.70, f32[1,2,128,128]{3,2,1,0:T(8,128)S(1)} %get-tuple-element.21), kind=kOutput, calls=%fused_computation.16 | convolution fusion | flops 806354944 | bytes 7405568 | tf_op jit(solution)/shard_map/dot_general | solution.py:69
  36.1 1.8 %fusion.71 = f32[2,16,128,128]{3,2,1,0:T(8,128)S(1)} fusion(f32[2,16,128,128]{3,2,1,0:T(8,128)S(1)} %add_multiply_fusion, f32[1,2,128,128]{3,2,1,0:T(8,128)S(1)} %get-tuple-element.21), kind=kOutput, calls=%fused_computation.95 | convolution fusion | flops 805306368 | bytes 4259840 | tf_op jit(solution)/shard_map/dot_general | solution.py:69
  37.9 1.8 %fusion.75 = f32[2,16,128,128]{3,2,1,0:T(8,128)S(1)} fusion(f32[2,16,128,128]{3,2,1,0:T(8,128)S(1)} %add_multiply_fusion, f32[1,2,128,128]{3,2,1,0:T(8,128)S(1)} %get-tuple-element.20), kind=kOutput, calls=%fused_computation.99 | convolution fusion | flops 805306368 | bytes 4259840 | tf_op jit(solution)/shard_map/dot_general | solution.py:69
  39.8 1.8 %fusion.10 = f32[2,16,128,256]{3,2,1,0:T(8,128)S(1)} fusion(f32[2,16,128,128]{3,2,1,0:T(8,128)S(1)} %fusion.72, f32[2,16,128,128]{3,2,1,0:T(8,128)S(1)} %fusion.75, s32[256]{0:T(256)S(1)} %get-tuple-element.24), kind=kOutput, calls=%fused_computation.14 | convolution fusion | flops 1611169792 | bytes 8389632 | tf_op jit(solution)/shard_map/dot_general | solution.py:69
  41.6 2.8 %add_reduce_fusion = (f32[2,16,256]{2,1,0:T(8,128)S(1)}, f32[2,16,256]{2,1,0:T(8,128)S(1)}) fusion(f32[2,16,128,256]{3,2,1,0:T(8,128)S(1)} %fusion.10, f32[128,256]{1,0:T(8,128)S(1)} %get-tuple-element.27, f32[128,256]{1,0:T(8,128)S(1)} %get-tuple-element.26, s32[256]{0:T(256)S(1)} %get-tuple-element.24, f32[2,16,128,128]{3,2,1,0:T(8,128)S(1)} %fusion.71, ...), kind=kOutput, calls=%fused_computation.1 | convolution fusion | flops 1619542016 | bytes 8717312 | tf_op jit(solution)/shard_map/dot_general | solution.py:69
  44.7 1.4 %reshape.232 = f32[8,1,2048]{2,1,0:T(1,128)} reshape(f32[256,2,2,16]{3,2,1,0:T(2,128)S(1)} %bitcast.152) | data formatting | bytes 131072
  46.1 3.4 %all-to-all-start.1 = ((f32[8,1,2048]{2,1,0:T(1,128)}), f32[8,1,2048]{2,1,0:T(1,128)S(1)}, u32[]{:S(2)}, u32[]{:S(2)}) async-start(f32[8,1,2048]{2,1,0:T(1,128)} %reshape.232), calls=%async_computation.1 | async-start | bytes 131072 | tf_op jit(solution)/shard_map/all_to_all | solution.py:92
  49.5 6.8 %all-to-all-done.1 = f32[8,1,2048]{2,1,0:T(1,128)S(1)} async-done(((f32[8,1,2048]{2,1,0:T(1,128)}), f32[8,1,2048]{2,1,0:T(1,128)S(1)}, u32[]{:S(2)}, u32[]{:S(2)}) %all-to-all-start.1) | async-done | bytes 65568 | tf_op jit(solution)/shard_map/all_to_all | solution.py:92
  56.3 0.8 reduce.1
  57.1 0.7 reshape.233
  58.8 3.3 %collective-permute-done = bf16[2,2,32,128]{3,2,0,1:T(8,128)(2,1)S(1)} collective-permute-done((bf16[2,2,32,128]{3,2,0,1:T(8,128)(2,1)S(1)}, bf16[2,2,32,128]{3,2,0,1:T(8,128)(2,1)S(1)}, u32[]{:S(2)}, u32[]{:S(2)}) %collective-permute-start) | collective-permute-done | bytes 32800 | tf_op jit(solution)/shard_map/ppermute | solution.py:12
  62.1 3.3 %collective-permute-done.1 = bf16[2,2,32,128]{3,2,0,1:T(8,128)(2,1)S(1)} collective-permute-done((bf16[2,2,32,128]{3,2,0,1:T(8,128)(2,1)S(1)}, bf16[2,2,32,128]{3,2,0,1:T(8,128)(2,1)S(1)}, u32[]{:S(2)}, u32[]{:S(2)}) %collective-permute-start.1) | collective-permute-done | bytes 32800 | tf_op jit(solution)/shard_map/ppermute | solution.py:12
  65.4 4.3 %fusion.90 = (bf16[1,256,32,128]{3,2,1,0:T(8,128)(2,1)S(1)}, bf16[1,256,32,128]{3,2,1,0:T(8,128)(2,1)}) fusion(bf16[2,256,32,128]{3,2,1,0:T(8,128)(2,1)} %param.5), kind=kLoop, calls=%fused_computation.143 | loop fusion | bytes 8388608 | tf_op jit(solution)/shard_map/slice | solution.py:71
  69.7 0.6 copy.81
  70.5 2.3 %fusion.26 = f32[8,256]{1,0:T(8,128)S(1)} fusion(bf16[1,256,32,128]{3,2,1,0:T(8,128)(2,1)} %get-tuple-element.15, bf16[8,32,128]{2,1,0:T(8,128)(2,1)S(1)} %get-tuple-element.17), kind=kOutput, calls=%fused_computation.34 | convolution fusion | flops 16777216 | bytes 2170880 | tf_op jit(solution)/shard_map/dot_general | solution.py:102
  72.8 0.7 fusion.25
  73.5 0.7 fusion.30
  74.2 0.7 fusion.32
  74.9 33.7 %psum.7 = f32[2,8,256]{2,1,0:T(8,128)S(1)} all-reduce(f32[2,8,256]{2,1,0:T(8,128)S(1)} %pad_maximum_fusion.5), channel_id=1, replica_groups=mesh['pw'=8,'band'=4] {'pw'}, use_global_device_ids=true, to_apply=%region_2.3 | all-reduce | flops 4096 | bytes 32768 | tf_op jit(solution)/shard_map/psum | solution.py:111
  108.5 0.6 constant_dynamic-slice_fusion
  (44 shorter events, 4.5 us)
Async XLA Ops:
  0.6 10.5 %copy-start.3 = (s32[256]{0:T(256)S(1)}, s32[256]{0:T(256)}, u32[]{:S(2)}) copy-start(s32[256]{0:T(256)} %param.7) | copy-start | bytes 3076
  0.6 11.0 %copy-start.1 = (f32[16,128,128]{2,1,0:T(8,128)S(1)}, f32[16,128,128]{2,1,0:T(8,128)}, u32[]{:S(2)}) copy-start(f32[16,128,128]{2,1,0:T(8,128)} %param.6) | copy-start | bytes 3145732
  3.8 14.2 %all-to-all-start = ((f32[8,1,2048]{2,1,0:T(1,128)}), f32[8,1,2048]{2,1,0:T(1,128)S(1)}, u32[]{:S(2)}, u32[]{:S(2)}) async-start(f32[8,1,2048]{2,1,0:T(1,128)} %reshape.230), calls=%async_computation | async-start | bytes 131072 | tf_op jit(solution)/shard_map/all_to_all | solution.py:76
  44.4 13.7 %copy-start.2 = (f32[2,2,32,128]{3,2,1,0:T(8,128)S(1)}, f32[2,2,32,128]{3,2,1,0:T(8,128)}, u32[]{:S(2)}) copy-start(f32[2,2,32,128]{3,2,1,0:T(8,128)} %param.4) | copy-start | bytes 196612
  46.1 10.2 %all-to-all-start.1 = ((f32[8,1,2048]{2,1,0:T(1,128)}), f32[8,1,2048]{2,1,0:T(1,128)S(1)}, u32[]{:S(2)}, u32[]{:S(2)}) async-start(f32[8,1,2048]{2,1,0:T(1,128)} %reshape.232), calls=%async_computation.1 | async-start | bytes 131072 | tf_op jit(solution)/shard_map/all_to_all | solution.py:92
  58.7 3.4 %collective-permute-start = (bf16[2,2,32,128]{3,2,0,1:T(8,128)(2,1)S(1)}, bf16[2,2,32,128]{3,2,0,1:T(8,128)(2,1)S(1)}, u32[]{:S(2)}, u32[]{:S(2)}) collective-permute-start(bf16[2,2,32,128]{3,2,0,1:T(8,128)(2,1)S(1)} %get-tuple-element.28), channel_id=1, source_target_pairs={{0,1},{1,2},{2,3},{3,0},{4,5},{5,6},{6,7},{7,4},{8,9},{9,10},{10,1... | collective-permute-start | bytes 98312 | tf_op jit(solution)/shard_map/ppermute | solution.py:12
  62.1 3.3 %collective-permute-start.1 = (bf16[2,2,32,128]{3,2,0,1:T(8,128)(2,1)S(1)}, bf16[2,2,32,128]{3,2,0,1:T(8,128)(2,1)S(1)}, u32[]{:S(2)}, u32[]{:S(2)}) collective-permute-start(bf16[2,2,32,128]{3,2,0,1:T(8,128)(2,1)S(1)} %collective-permute-done), channel_id=1, source_target_pairs={{0,1},{1,2},{2,3},{3,0},{4,5},{5,6},{6,7},{7,4},{8,9},{9,10},{10,1... | collective-permute-start | bytes 98312 | tf_op jit(solution)/shard_map/ppermute | solution.py:12
  65.4 4.9 %collective-permute-start.2 = (bf16[2,2,32,128]{3,2,0,1:T(8,128)(2,1)S(1)}, bf16[2,2,32,128]{3,2,0,1:T(8,128)(2,1)S(1)}, u32[]{:S(2)}, u32[]{:S(2)}) collective-permute-start(bf16[2,2,32,128]{3,2,0,1:T(8,128)(2,1)S(1)} %collective-permute-done.1), channel_id=1, source_target_pairs={{0,1},{1,2},{2,3},{3,0},{4,5},{5,6},{6,7},{7,4},{8,9},{9,10},{10,1... | collective-permute-start | bytes 98312 | tf_op jit(solution)/shard_map/ppermute | solution.py:12
  69.7 3.1 %copy-start = (bf16[1,256,32,128]{3,2,1,0:T(8,128)(2,1)S(1)}, bf16[1,256,32,128]{3,2,1,0:T(8,128)(2,1)}, u32[]{:S(2)}) copy-start(bf16[1,256,32,128]{3,2,1,0:T(8,128)(2,1)} %get-tuple-element.15) | copy-start | bytes 6291460
